TPU v7x, 256 devices: a whole 4x4x8 slice. The times are simulated.
256 devices in a mesh: tile: 16 (over z, x_lo), obj: 16 (over x_hi, y, core).
Axes of the slice: x: 4 (x_hi: 2, x_lo: 2; x = x_hi * 2 + x_lo), y: 4, z: 8, core: 2. Of those that a mesh axis runs over, the one named last changes fastest.
Arguments:
- adjoint_in: float32 [256, 2, 256, 1024], P('obj', None, 'tile'), may hold values from -6 to 6
- checkpoint_store: float32 [64, 2, 256, 1024], P('obj', None, 'tile'), may hold values from 1900 to 2500, as said below
- interval: int32 [1], replicated, may hold values from 0 to 63
- sea_mask: int32 [256, 1024], P('tile'), may hold values 0 or 1
- zonal_speed: float32 [256, 1024], P('tile'), may hold values from -0.45 to 0.45
- mixing: float32 [256, 1024], P('tile'), may hold values from 0.02 to 0.2
- piston: float32 [256, 32], P('tile'), may hold values from 0.1 to 0.9
- cell_area: float32 [256, 32], P('tile'), may hold values from 5 to 50
- region: int32 [256, 32], P('tile'), may hold values from 0 to 255
Outputs:
- adjoint_out: float32 [256, 2, 256, 1024], P('obj', None, 'tile')
Inputs may be any that keep to these rules, and one draw needn't show every extreme that they name: region numbers name objectives. `checkpoint_store`: dissolved carbon lies in 1900 to 2100 and alkalinity exceeds it by 200 to 400 in every cell.
All inputs are finite; a program needn't handle non-finite values. No bound on the sum of `sea_mask` on one device may be relied on, other than what follows from the above.
Results may differ from a plain program's by a relative error of at most 0.0003.
Values sent between devices are 32-bit elements; how exact they have to be, the bound alone decides.
No kernel may reach another device: no remote copies, remote signals or barrier semaphores. Data moves between devices by JAX's collectives and lax.ppermute only.
A program may use at most 64 MiB of HBM per device.

v0:
```python
import jax
import jax.numpy as jnp
from jax import lax
from jax.sharding import PartitionSpec as P

ROWS = 32
LEVELS = 32
NEWTON = 4
DISSOCIATION_ONE = 1400.0
DISSOCIATION_TWO = 1.1
BORATE_CONSTANT = 2.5
BORON_TOTAL = 416.0
AIR_CARBON = 14.0
START_HYDROGEN = 2.0
ROW_DIFFUSION = 0.1


def padded(cells, sides, width):
    for axis, dim in sides:
        count = lax.axis_size(axis)
        head = lax.slice_in_dim(cells, 0, width, axis=dim)
        tail = lax.slice_in_dim(cells, cells.shape[dim] - width, cells.shape[dim], axis=dim)
        cells = jnp.concatenate(
            [
                lax.ppermute(tail, axis, [(i, (i + 1) % count) for i in range(count)]),
                cells,
                lax.ppermute(head, axis, [((i + 1) % count, i) for i in range(count)]),
            ],
            axis=dim,
        )
    return cells


def spread(value, axis, source):
    kept = jnp.where(lax.axis_index(axis) == source, value, 0).astype(value.dtype)
    return lax.psum(kept, axis)


def chemistry(carbon, alkalinity, piston, surface_sea):
    hydrogen = jnp.full_like(carbon, START_HYDROGEN)
    for iteration in range(NEWTON):
        square = hydrogen * hydrogen
        denominator = square + DISSOCIATION_ONE * hydrogen + DISSOCIATION_ONE * DISSOCIATION_TWO
        carbonate = carbon * DISSOCIATION_ONE * (hydrogen + 2.0 * DISSOCIATION_TWO) / denominator
        borate = BORON_TOTAL * BORATE_CONSTANT / (hydrogen + BORATE_CONSTANT)
        derivative = -carbon * DISSOCIATION_ONE * (
            square + 4.0 * DISSOCIATION_TWO * hydrogen + DISSOCIATION_ONE * DISSOCIATION_TWO
        ) / (denominator * denominator) - borate / (hydrogen + BORATE_CONSTANT)
        hydrogen = hydrogen - (carbonate + borate - alkalinity) / derivative
    square = hydrogen * hydrogen
    denominator = square + DISSOCIATION_ONE * hydrogen + DISSOCIATION_ONE * DISSOCIATION_TWO
    dissolved = carbon * square / denominator
    return surface_sea * piston * (AIR_CARBON - dissolved)


def forward_shift(source, offset):
    padding = jnp.zeros(source.shape[:-1] + (offset,), source.dtype)
    return jnp.concatenate([source[..., offset:], padding], axis=-1)


def backward_shift(source, offset):
    padding = jnp.zeros(source.shape[:-1] + (offset,), source.dtype)
    return jnp.concatenate([padding, source[..., :-offset]], axis=-1)


def column_weights(sea_float, mixing):
    cell_index = jnp.arange(LEVELS * ROWS, dtype=jnp.int32)
    row_open = (cell_index % ROWS < ROWS - 1).astype(jnp.float32)
    level_open = (cell_index // ROWS < LEVELS - 1).astype(jnp.float32)
    row_weight = ROW_DIFFUSION * row_open * sea_float * forward_shift(sea_float, 1)
    level_weight = mixing * level_open * sea_float * forward_shift(sea_float, ROWS)
    return (row_weight, level_weight)


def column_mix(source, row_weight, level_weight):
    row_flux = row_weight * (forward_shift(source, 1) - source)
    level_flux = level_weight * (forward_shift(source, ROWS) - source)
    return row_flux - backward_shift(row_flux, 1) + level_flux - backward_shift(level_flux, ROWS)


def zonal_weights(sea_float, sea_east, velocity):
    opened = sea_float * sea_east
    magnitude = jnp.abs(velocity)
    return jnp.stack(
        [
            opened * (-velocity - magnitude) / 12.0,
            opened * (7.0 * velocity + 3.0 * magnitude) / 12.0,
            opened * (7.0 * velocity - 3.0 * magnitude) / 12.0,
            opened * (magnitude - velocity) / 12.0,
        ]
    )


def trim_rim(source, keep_rim, outer_rim, dimension):
    length = source.shape[dimension] - 2 * outer_rim
    return lax.slice_in_dim(
        source, outer_rim - keep_rim, outer_rim + length + keep_rim, axis=dimension
    )


def surface_slopes(carbon, alkalinity, piston, surface_sea):

    def uptake_of(carbon_in, alkalinity_in):
        return chemistry(carbon_in, alkalinity_in, piston, surface_sea)

    uptake, pullback = jax.vjp(uptake_of, carbon, alkalinity)
    by_carbon, by_alkalinity = pullback(jnp.ones_like(carbon))
    return (uptake, jnp.stack([by_carbon, by_alkalinity]))


def advance_rim(extended, weights, row_weight, level_weight, uptake):
    length = extended.shape[1]
    face_flux = (
        weights[0, 1 : length - 2] * extended[:, 0 : length - 3]
        + weights[1, 1 : length - 2] * extended[:, 1 : length - 2]
        + weights[2, 1 : length - 2] * extended[:, 2 : length - 1]
        + weights[3, 1 : length - 2] * extended[:, 3:length]
    )
    interior = extended[:, 2 : length - 2]
    zonal_term = -(face_flux[:, 1:] - face_flux[:, :-1])
    transported = interior + zonal_term + column_mix(interior, row_weight, level_weight)
    surface_row = transported[0, :, :ROWS] + uptake
    carbon = jnp.concatenate([surface_row, transported[0, :, ROWS:]], axis=-1)
    return jnp.stack([carbon, transported[1]])


def retreat(extended, weights, row_weight, level_weight, slopes, objective_seeds):
    length = extended.shape[2]
    difference = extended[:, :, 1:] - extended[:, :, :-1]
    zonal_term = (
        weights[0, 3 : length - 1] * difference[:, :, 3 : length - 1]
        + weights[1, 2 : length - 2] * difference[:, :, 2 : length - 2]
        + weights[2, 1 : length - 3] * difference[:, :, 1 : length - 3]
        + weights[3, 0 : length - 4] * difference[:, :, 0 : length - 4]
    )
    interior = extended[:, :, 2 : length - 2]
    adjoint = interior + zonal_term + column_mix(interior, row_weight, level_weight)
    forcing = interior[:, 0, :, :ROWS] + objective_seeds
    surface = adjoint[..., :ROWS] + slopes[None] * forcing[:, None]
    return jnp.concatenate([surface, adjoint[..., ROWS:]], axis=-1)


def body(
    adjoint_in, checkpoint_store, interval, sea_mask, zonal_speed, mixing, piston, cell_area, region
):
    groups = adjoint_in.shape[0]
    cell_count = adjoint_in.shape[3]
    rim_depth = 2
    statics = jnp.concatenate(
        [
            sea_mask.astype(jnp.float32),
            zonal_speed,
            mixing,
            piston,
            cell_area,
            region.astype(jnp.float32),
        ],
        axis=1,
    )
    widened = padded(statics, (("tile", 0),), rim_depth)
    sea_wide = widened[:, :cell_count]
    speed_wide = widened[:, cell_count : 2 * cell_count]
    mixing_wide = widened[:, 2 * cell_count : 3 * cell_count]
    offset = 3 * cell_count
    piston_wide = widened[:, offset : offset + ROWS]
    area_wide = widened[:, offset + ROWS : offset + 2 * ROWS]
    region_wide = widened[:, offset + 2 * ROWS : offset + 3 * ROWS]
    sea_east = jnp.concatenate([sea_wide[1:], jnp.zeros_like(sea_wide[:1])], axis=0)
    weights = zonal_weights(sea_wide, sea_east, speed_wide)
    row_weight, level_weight = column_weights(sea_wide, mixing_wide)
    surface_sea = sea_wide[:, :ROWS]
    targets = (lax.axis_index("obj") * groups + jnp.arange(groups, dtype=jnp.int32)).astype(
        jnp.float32
    )
    objective_seeds = area_wide[None] * (region_wide[None] == targets[:, None, None]).astype(
        jnp.float32
    )
    owners = lax.axis_size("obj")
    owner_index = interval[0] % owners
    stored = lax.dynamic_index_in_dim(checkpoint_store, interval[0] // owners, 0, keepdims=False)
    linearize_extended = padded(spread(stored, "obj", owner_index), (("tile", 1),), rim_depth)
    inner_rim = rim_depth - 2
    piston_inner = trim_rim(piston_wide, inner_rim, rim_depth, 0)
    sea_inner = trim_rim(surface_sea, inner_rim, rim_depth, 0)
    initial_inner = trim_rim(linearize_extended, inner_rim, rim_depth, 1)
    uptake_first, slopes_first = surface_slopes(
        initial_inner[0, :, :ROWS], initial_inner[1, :, :ROWS], piston_inner, sea_inner
    )
    following = advance_rim(
        linearize_extended,
        weights,
        trim_rim(row_weight, inner_rim, rim_depth, 0),
        trim_rim(level_weight, inner_rim, rim_depth, 0),
        uptake_first,
    )
    _, slopes_second = surface_slopes(
        following[0, :, :ROWS], following[1, :, :ROWS], piston_inner, sea_inner
    )
    slopes = jnp.stack([slopes_first, slopes_second])
    adjoint = adjoint_in
    for substep in (1, 0):
        extended = padded(adjoint, (("tile", 2),), 2)
        rim_in = 0 + 2
        adjoint = retreat(
            extended,
            trim_rim(weights, rim_in, rim_depth, 1),
            trim_rim(row_weight, 0, rim_depth, 0),
            trim_rim(level_weight, 0, rim_depth, 0),
            trim_rim(slopes[substep], 0, rim_depth - 2, 1),
            trim_rim(objective_seeds, 0, rim_depth, 1),
        )
    return adjoint


def solution(mesh):
    placed = (
        P("obj", None, "tile", None),
        P("obj", None, "tile", None),
        P(),
        P("tile", None),
        P("tile", None),
        P("tile", None),
        P("tile", None),
        P("tile", None),
        P("tile", None),
    )
    return jax.shard_map(
        body, mesh=mesh, in_specs=placed, out_specs=P("obj", None, "tile", None), check_vma=False
    )
```

profile of v0, /device:TPU:1, one launch (start us, length us, event | category | flops | bytes accessed | tf_op | source)
XLA Modules:
  0.0 209.7 jit_solution(15050452365637785768)
XLA Ops:
  6.5 0.0 all-reduce.17.cloned.1.call-start
  7.2 1.6 select_bitcast_fusion
  8.8 0.0 all-reduce.17.cloned.1.call-update
  8.8 0.7 convert_element_type.25
  9.5 0.8 convert_element_type.24
  10.4 1.0 concatenate.75
  11.3 2.1 %collective-permute-start = (f32[2,3168]{1,0:T(2,128)S(1)}, f32[2,3168]{1,0:T(2,128)S(1)}, u32[]{:S(2)}, u32[]{:S(2)}) collective-permute-start(f32[2,3168]{1,0:T(2,128)S(1)} %get-tuple-element.39), channel_id=1, source_target_pairs={{0,16},{16,32},{32,48},{48,64},{64,80},{80,96},{96,112},{112,128},... | collective-permute-start | bytes 76040 | tf_op jit(solution)/shard_map/ppermute | solution.py:25
  13.4 5.4 %collective-permute-start.1 = (f32[2,3168]{1,0:T(2,128)S(1)}, f32[2,3168]{1,0:T(2,128)S(1)}, u32[]{:S(2)}, u32[]{:S(2)}) collective-permute-start(f32[2,3168]{1,0:T(2,128)S(1)} %get-tuple-element.40), channel_id=1, source_target_pairs={{16,0},{32,16},{48,32},{64,48},{80,64},{96,80},{112,96},{128,112},... | collective-permute-start | bytes 76040 | tf_op jit(solution)/shard_map/ppermute | solution.py:27
  18.8 2.8 %copy.14 = f32[16,2,16,1024]{3,0,2,1:T(8,128)S(1)} copy(f32[16,2,16,1024]{3,2,1,0:T(8,128)} %param.9) | data formatting | bytes 4194304 | tf_op args[0]
  21.6 0.9 fusion.63
  22.5 1.4 collective-permute-start.3
  23.9 0.1 collective-permute-start.2
  24.0 2.0 slice.328
  25.9 1.9 slice.322
  27.9 0.0 collective-permute-done
  27.9 0.0 collective-permute-done.1
  27.9 0.1 slice.320
  28.0 0.1 slice.325
  28.1 0.1 multiply_bitcast_fusion.1
  28.2 0.0 copy-start.3
  28.3 0.1 pad_maximum_fusion.8
  28.4 0.1 select_add_fusion
  28.6 133.8 %all-reduce.17.cloned.1.call-done = f32[2,16,1024]{2,1,0:T(8,128)} async-done(((f32[2,16,1024]{2,1,0:T(8,128)}), f32[2,16,1024]{2,1,0:T(8,128)}) %all-reduce.17.cloned.1.call-update) | async-done | bytes 131088 | tf_op jit(solution)/shard_map/psum | solution.py:36
  162.3 0.9 fusion.65
  163.3 0.4 collective-permute-start.4
  163.6 3.3 %collective-permute-start.5 = (f32[2,2,1024]{2,1,0:T(2,128)S(1)}, f32[2,2,1024]{2,1,0:T(2,128)S(1)}, u32[]{:S(2)}, u32[]{:S(2)}) collective-permute-start(f32[2,2,1024]{2,1,0:T(2,128)S(1)} %get-tuple-element.47), channel_id=1, source_target_pairs={{16,0},{32,16},{48,32},{64,48},{80,64},{96,80},{112,96},{128,112},... | collective-permute-start | bytes 49160 | tf_op jit(solution)/shard_map/ppermute | solution.py:27
  166.9 1.0 slice.346
  167.9 1.0 slice.344
  168.9 0.0 copy-start
  168.9 0.0 copy-start.1
  168.9 1.1 subtract_multiply_fusion.5
  170.0 0.0 copy-done.3
  170.1 1.1 add_bitcast_fusion.1
  171.1 0.0 collective-permute-done.5
  171.1 0.0 collective-permute-done.4
  171.2 1.1 fusion.13
  172.2 0.0 copy-done.2
  172.3 0.1 fusion.19
  172.4 0.1 slice_bitcast_fusion.6
  172.5 0.1 add_bitcast_fusion
  172.5 0.1 maximum_bitcast_fusion
  172.6 0.1 add_bitcast_fusion.3
  172.8 0.0 collective-permute-done.2
  172.9 0.0 copy-done
  172.9 0.0 copy-done.1
  172.9 3.5 %subtract_multiply_fusion.3 = (f32[16,2,16,1024]{3,0,2,1:T(8,128)S(1)}, f32[16,2,20,1024]{3,0,2,1:T(8,128)S(1)}, f32[16,2,16,1024]{3,0,2,1:T(8,128)S(1)}) fusion(f32[16,2,16,1023]{3,0,2,1:T(8,128)} %slice.322, f32[16,1024]{1,0:T(8,128)S(1)} %get-tuple-element.48, f32[16,2,16,1024]{3,2,1,0:T(8,128)S(1)} %copy-done, ...), kind=kLoop, calls=%fused_computation.30 | loop fusion | flops 2097152 | bytes 12711936 | tf_op jit(solution)/shard_map/mul | solution.py:76
  176.4 0.0 collective-permute-done.3
  176.4 0.3 slice_subtract_fusion.1
  176.8 4.4 %fusion.8 = f32[16,2,16,1024]{3,0,2,1:T(8,128)S(1)} fusion(f32[16,2,19,1024]{3,0,2,1:T(8,128)S(1)} %slice_subtract_fusion.1, f32[16,2,16,992]{3,0,2,1:T(8,128)S(1)} %bitcast.349, f32[16,2,16,1024]{3,0,2,1:T(8,128)S(1)} %get-tuple-element.29, f32[16,2,16,1024]{3,0,2,1:T(8,128)S(1)} %get-tuple-element.27, f32[16,2,16,1023]{3,0,2,1:T(8,128)S(1)} %bitcast.348, ...), kind=kLoop, calls=%fused_computation.20 | loop fusion | flops 6291456 | bytes 21166080 | tf_op jit(solution)/shard_map/add | solution.py:137
  181.2 0.6 slice.357
  181.9 0.2 fusion.11
  182.1 0.7 fusion
  182.8 0.1 collective-permute-start.6
  182.8 3.6 %collective-permute-start.7 = (f32[16,2,2,1024]{3,0,2,1:T(8,128)S(1)}, f32[16,2,2,1024]{3,0,2,1:T(8,128)S(1)}, u32[]{:S(2)}, u32[]{:S(2)}) collective-permute-start(f32[16,2,2,1024]{3,0,2,1:T(8,128)S(1)} %get-tuple-element.26), channel_id=1, source_target_pairs={{16,0},{32,16},{48,32},{64,48},{80,64},{96,80},{112,96},{128,112},... | collective-permute-start | bytes 786440 | tf_op jit(solution)/shard_map/ppermute | solution.py:27
  186.4 1.2 subtract_multiply_fusion.1
  187.7 0.1 select_add_fusion.1
  187.7 5.3 %collective-permute-done.6 = f32[16,2,2,1024]{3,0,2,1:T(8,128)S(1)} collective-permute-done((f32[16,2,2,1024]{3,0,2,1:T(8,128)S(1)}, f32[16,2,2,1024]{3,0,2,1:T(8,128)S(1)}, u32[]{:S(2)}, u32[]{:S(2)}) %collective-permute-start.6) | collective-permute-done | bytes 262176 | tf_op jit(solution)/shard_map/ppermute | solution.py:25
  193.1 2.2 %collective-permute-done.7 = f32[16,2,2,1024]{3,0,2,1:T(8,128)S(1)} collective-permute-done((f32[16,2,2,1024]{3,0,2,1:T(8,128)S(1)}, f32[16,2,2,1024]{3,0,2,1:T(8,128)S(1)}, u32[]{:S(2)}, u32[]{:S(2)}) %collective-permute-start.7) | collective-permute-done | bytes 262176 | tf_op jit(solution)/shard_map/ppermute | solution.py:27
  195.3 0.6 pad_maximum_fusion.1
  195.9 0.2 slice_subtract_fusion
  196.1 2.9 %fusion.3 = f32[16,2,16,1024]{3,0,2,1:T(8,128)S(1)} fusion(f32[16,2,19,1024]{3,0,2,1:T(8,128)S(1)} %slice_subtract_fusion, f32[16,2,16,992]{3,0,2,1:T(8,128)S(1)} %bitcast.350, f32[16,2,16,1024]{3,0,2,1:T(8,128)S(1)} %get-tuple-element.23, f32[16,2,16,1023]{3,0,2,1:T(8,128)S(1)} %bitcast.347, f32[16,2,16,992]{3,0,2,1:T(8,128)S(1)} %slice.357, ...), kind=kLoop, calls=%fused_computation.11 | loop fusion | flops 7864320 | bytes 19134464 | tf_op jit(solution)/shard_map/add | solution.py:137
  199.1 0.6 slice.374
  199.8 0.6 pad_maximum_fusion.2
  200.4 2.5 %copy.20 = f32[16,2,16,1024]{3,2,1,0:T(8,128)} copy(f32[16,2,16,1024]{3,0,2,1:T(8,128)S(1)} %pad_maximum_fusion.2) | data formatting | bytes 4194304 | tf_op jit(solution)/shard_map/concatenate | solution.py:140
  (23 shorter events, 0.4 us)
Async XLA Ops:
  6.5 155.8 %all-reduce.17.cloned.1.call-start = ((), (), s32[]{:S(2)}) async-start(), calls=%async_computation | async-start | bytes 262144 | tf_op jit(solution)/shard_map/psum | solution.py:36
  11.3 16.5 %collective-permute-start = (f32[2,3168]{1,0:T(2,128)S(1)}, f32[2,3168]{1,0:T(2,128)S(1)}, u32[]{:S(2)}, u32[]{:S(2)}) collective-permute-start(f32[2,3168]{1,0:T(2,128)S(1)} %get-tuple-element.39), channel_id=1, source_target_pairs={{0,16},{16,32},{32,48},{48,64},{64,80},{80,96},{96,112},{112,128},... | collective-permute-start | bytes 76040 | tf_op jit(solution)/shard_map/ppermute | solution.py:25
  13.4 14.4 %collective-permute-start.1 = (f32[2,3168]{1,0:T(2,128)S(1)}, f32[2,3168]{1,0:T(2,128)S(1)}, u32[]{:S(2)}, u32[]{:S(2)}) collective-permute-start(f32[2,3168]{1,0:T(2,128)S(1)} %get-tuple-element.40), channel_id=1, source_target_pairs={{16,0},{32,16},{48,32},{64,48},{80,64},{96,80},{112,96},{128,112},... | collective-permute-start | bytes 76040 | tf_op jit(solution)/shard_map/ppermute | solution.py:27
  22.5 153.9 %collective-permute-start.3 = (f32[16,2,2,1024]{3,0,2,1:T(8,128)}, f32[16,2,2,1024]{3,0,2,1:T(8,128)S(1)}, u32[]{:S(2)}, u32[]{:S(2)}) collective-permute-start(f32[16,2,2,1024]{3,0,2,1:T(8,128)} %get-tuple-element.30), channel_id=1, source_target_pairs={{16,0},{32,16},{48,32},{64,48},{80,64},{96,80},{112,96},{128,112},... | collective-permute-start | bytes 786440 | tf_op jit(solution)/shard_map/ppermute | solution.py:27
  23.9 149.0 %collective-permute-start.2 = (f32[16,2,2,1024]{3,0,2,1:T(8,128)}, f32[16,2,2,1024]{3,0,2,1:T(8,128)S(1)}, u32[]{:S(2)}, u32[]{:S(2)}) collective-permute-start(f32[16,2,2,1024]{3,0,2,1:T(8,128)} %get-tuple-element.31), channel_id=1, source_target_pairs={{0,16},{16,32},{32,48},{48,64},{64,80},{80,96},{96,112},{112,128},... | collective-permute-start | bytes 786440 | tf_op jit(solution)/shard_map/ppermute | solution.py:25
  28.2 141.8 %copy-start.3 = (f32[16,32]{1,0:T(8,128)S(1)}, f32[16,32]{1,0:T(8,128)}, u32[]{:S(2)}) copy-start(f32[16,32]{1,0:T(8,128)} %param.15) | copy-start | bytes 6148
  162.3 9.9 %copy-start.2 = (f32[2,16,1024]{2,1,0:T(8,128)S(1)}, f32[2,16,1024]{2,1,0:T(8,128)}, u32[]{:S(2)}) copy-start(f32[2,16,1024]{2,1,0:T(8,128)} %all-reduce.17.cloned.1.call-done) | copy-start | bytes 393220
  163.3 7.9 %collective-permute-start.4 = (f32[2,2,1024]{2,1,0:T(2,128)S(1)}, f32[2,2,1024]{2,1,0:T(2,128)S(1)}, u32[]{:S(2)}, u32[]{:S(2)}) collective-permute-start(f32[2,2,1024]{2,1,0:T(2,128)S(1)} %get-tuple-element.46), channel_id=1, source_target_pairs={{0,16},{16,32},{32,48},{48,64},{64,80},{80,96},{96,112},{112,128},... | collective-permute-start | bytes 49160 | tf_op jit(solution)/shard_map/ppermute | solution.py:25
  163.6 7.5 %collective-permute-start.5 = (f32[2,2,1024]{2,1,0:T(2,128)S(1)}, f32[2,2,1024]{2,1,0:T(2,128)S(1)}, u32[]{:S(2)}, u32[]{:S(2)}) collective-permute-start(f32[2,2,1024]{2,1,0:T(2,128)S(1)} %get-tuple-element.47), channel_id=1, source_target_pairs={{16,0},{32,16},{48,32},{64,48},{80,64},{96,80},{112,96},{128,112},... | collective-permute-start | bytes 49160 | tf_op jit(solution)/shard_map/ppermute | solution.py:27
  168.9 4.0 %copy-start = (f32[16,2,16,1024]{3,2,1,0:T(8,128)S(1)}, f32[16,2,16,1024]{3,2,1,0:T(8,128)}, u32[]{:S(2)}) copy-start(f32[16,2,16,1024]{3,2,1,0:T(8,128)} %param.9) | copy-start | bytes 6291460
  168.9 3.9 %copy-start.1 = (f32[16,2,16,992]{3,0,2,1:T(8,128)S(1)}, f32[16,2,16,992]{3,0,2,1:T(8,128)}, u32[]{:S(2)}) copy-start(f32[16,2,16,992]{3,0,2,1:T(8,128)} %slice.328) | copy-start | bytes 6094852
  182.8 10.3 %collective-permute-start.6 = (f32[16,2,2,1024]{3,0,2,1:T(8,128)S(1)}, f32[16,2,2,1024]{3,0,2,1:T(8,128)S(1)}, u32[]{:S(2)}, u32[]{:S(2)}) collective-permute-start(f32[16,2,2,1024]{3,0,2,1:T(8,128)S(1)} %get-tuple-element.25), channel_id=1, source_target_pairs={{0,16},{16,32},{32,48},{48,64},{64,80},{80,96},{96,112},{112,128},... | collective-permute-start | bytes 786440 | tf_op jit(solution)/shard_map/ppermute | solution.py:25
  182.8 12.4 %collective-permute-start.7 = (f32[16,2,2,1024]{3,0,2,1:T(8,128)S(1)}, f32[16,2,2,1024]{3,0,2,1:T(8,128)S(1)}, u32[]{:S(2)}, u32[]{:S(2)}) collective-permute-start(f32[16,2,2,1024]{3,0,2,1:T(8,128)S(1)} %get-tuple-element.26), channel_id=1, source_target_pairs={{16,0},{32,16},{48,32},{64,48},{80,64},{96,80},{112,96},{128,112},... | collective-permute-start | bytes 786440 | tf_op jit(solution)/shard_map/ppermute | solution.py:27
Sparse Core Ops, SparseCore 0:
  9.9 152.3 all-reduce.16
where the time goes:
time: 210 us
  waiting for transfers between devices  141 us (67%)
  other arithmetic  22.1 us (11%)
  starting transfers between devices  16.3 us (8%)
  local copies, waits for them, and re-layouts  15.6 us (7%)
  between operations  14.4 us (7%)
    psum x1, waiting for transfers between devices, spread(): return lax.psum(kept, axis)  134 us
    ppermute x4, starting transfers between devices, padded(): lax.ppermute(head, axis, [((i + 1) % count, i) for i in range(count)])  13.6 us
    add x2, other arithmetic, retreat(): interior + zonal_term + column_mix(interior, row_weight, level_weight)  7.35 us
    slice x6, local copies, waits for them, and re-layouts, forward_shift(): return jnp.concatenate([source[..., offset:], padding], axis=-1)  6.04 us
    mul x3, other arithmetic, column_mix(): row_flux = row_weight * (forward_shift(source, 1) - source)  5.84 us
    ppermute x4, waiting for transfers between devices, padded(): lax.ppermute(tail, axis, [(i, (i + 1) % count) for i in range(count)])  5.32 us
  transfers between devices with their start and end apart: 9, of which 3 were waited for; matrix products, arithmetic and copies ran while one was open for 11% of the time, Pallas kernels for 0%

commit v1 on v0

--- a/solution.py
+++ b/solution.py
@@ -33,7 +33,7 @@
 
 def spread(value, axis, source):
     kept = jnp.where(lax.axis_index(axis) == source, value, 0).astype(value.dtype)
-    return lax.psum(kept, axis)
+    return jnp.sum(lax.all_gather(kept, axis), 0)
 
 
 def chemistry(carbon, alkalinity, piston, surface_sea):

time: 210 us -> 109 us (0.52)
  waiting for transfers between devices: 141 us -> 45.8 us
  local copies, waits for them, and re-layouts: 15.6 us -> 12.4 us
  other arithmetic: 22.1 us -> 19.8 us
    psum x1 -> x0, waiting for transfers between devices: 134 us -> none  [spread(): return lax.psum(kept, axis)]
    all_gather x0 -> x1, waiting for transfers between devices: none -> 28.3 us  [spread(): return jnp.sum(lax.all_gather(kept, axis), 0)]
    ppermute x4, waiting for transfers between devices: 5.32 us -> 14.9 us  [padded(): lax.ppermute(tail, axis, [(i, (i + 1) % count) for i in range(count)])]
    slice x6, local copies, waits for them, and re-layouts: 6.04 us -> 1.57 us  [forward_shift(): return jnp.concatenate([source[..., offset:], padding], axis=-1)]
    mul x3, other arithmetic: 5.84 us -> 3 us  [column_mix(): row_flux = row_weight * (forward_shift(source, 1) - source)]
    unnamed x10 -> x8, local copies, waits for them, and re-layouts: 2.85 us -> 5.1 us
  transfers between devices with their start and end apart: 9 -> 9, of which waited for: 3 -> 6; matrix products, arithmetic and copies ran while one was open for 11% -> 16% of each run, Pallas kernels for 0% -> 0%
where the time goes in v1:
time: 109 us
  waiting for transfers between devices  45.8 us (42%)
  other arithmetic  19.8 us (18%)
  starting transfers between devices  16.5 us (15%)
  between operations  14.4 us (13%)
  local copies, waits for them, and re-layouts  12.4 us (11%)
    all_gather x1, waiting for transfers between devices, spread(): return jnp.sum(lax.all_gather(kept, axis), 0)  28.3 us
    ppermute x4, waiting for transfers between devices, padded(): lax.ppermute(tail, axis, [(i, (i + 1) % count) for i in range(count)])  14.9 us
    ppermute x4, starting transfers between devices, padded(): lax.ppermute(head, axis, [((i + 1) % count, i) for i in range(count)])  12.5 us
    add x2, other arithmetic, retreat(): interior + zonal_term + column_mix(interior, row_weight, level_weight)  7.13 us
    unnamed x8, local copies, waits for them, and re-layouts  5.1 us
    ppermute x4, starting transfers between devices, padded(): lax.ppermute(tail, axis, [(i, (i + 1) % count) for i in range(count)])  4.06 us
    mul x3, other arithmetic, column_mix(): row_flux = row_weight * (forward_shift(source, 1) - source)  3 us
    ppermute x4, waiting for transfers between devices, padded(): lax.ppermute(head, axis, [((i + 1) % count, i) for i in range(count)])  2.6 us
  transfers between devices with their start and end apart: 9, of which 6 were waited for; matrix products, arithmetic and copies ran while one was open for 16% of the time, Pallas kernels for 0%

profile of v1, /device:TPU:1, one launch (start us, length us, event | category | flops | bytes accessed | tf_op | source)
XLA Modules:
  0.0 108.9 jit_solution(2242174303969272847)
XLA Ops:
  6.5 0.0 all-gather.2.cloned.1.call-start
  7.2 1.6 %dynamic-slice_select_fusion = f32[1,2,16,1024]{3,2,1,0:T(8,128)} fusion(f32[4,2,16,1024]{3,2,1,0:T(8,128)} %param.10, s32[]{:T(128)S(6)} %select_n.48, pred[]{:T(512)S(6)} %eq.20), kind=kLoop, calls=%fused_computation.60 | loop fusion | flops 32768 | bytes 262149 | tf_op jit(solution)/shard_map/jit(_where)/select_n | solution.py:35
  8.8 0.0 all-gather.2.cloned.1.call-update
  8.8 0.7 convert_element_type.25
  9.5 0.8 convert_element_type.24
  10.4 1.0 concatenate.75
  11.3 2.1 %collective-permute-start = (f32[2,3168]{1,0:T(2,128)S(1)}, f32[2,3168]{1,0:T(2,128)S(1)}, u32[]{:S(2)}, u32[]{:S(2)}) collective-permute-start(f32[2,3168]{1,0:T(2,128)S(1)} %get-tuple-element.39), channel_id=1, source_target_pairs={{0,16},{16,32},{32,48},{48,64},{64,80},{80,96},{96,112},{112,128},... | collective-permute-start | bytes 76040 | tf_op jit(solution)/shard_map/ppermute | solution.py:25
  13.4 5.4 %collective-permute-start.1 = (f32[2,3168]{1,0:T(2,128)S(1)}, f32[2,3168]{1,0:T(2,128)S(1)}, u32[]{:S(2)}, u32[]{:S(2)}) collective-permute-start(f32[2,3168]{1,0:T(2,128)S(1)} %get-tuple-element.40), channel_id=1, source_target_pairs={{16,0},{32,16},{48,32},{64,48},{80,64},{96,80},{112,96},{128,112},... | collective-permute-start | bytes 76040 | tf_op jit(solution)/shard_map/ppermute | solution.py:27
  18.8 2.8 %copy.14 = f32[16,2,16,1024]{3,0,2,1:T(8,128)S(1)} copy(f32[16,2,16,1024]{3,2,1,0:T(8,128)} %param.9) | data formatting | bytes 4194304 | tf_op args[0]
  21.6 0.8 fusion.64
  22.5 1.4 %collective-permute-start.3 = (f32[16,2,2,1024]{3,0,2,1:T(8,128)}, f32[16,2,2,1024]{3,0,2,1:T(8,128)S(1)}, u32[]{:S(2)}, u32[]{:S(2)}) collective-permute-start(f32[16,2,2,1024]{3,0,2,1:T(8,128)} %get-tuple-element.30), channel_id=1, source_target_pairs={{16,0},{32,16},{48,32},{64,48},{80,64},{96,80},{112,96},{128,112},... | collective-permute-start | bytes 786440 | tf_op jit(solution)/shard_map/ppermute | solution.py:27
  23.8 0.1 collective-permute-start.2
  23.9 0.6 slice.328
  24.5 0.6 slice.322
  25.2 0.0 collective-permute-done
  25.2 0.0 collective-permute-done.1
  25.2 0.1 slice.320
  25.3 0.1 slice.325
  25.4 0.0 copy-start
  25.4 0.1 pad_maximum_fusion.9
  25.6 0.1 multiply_bitcast_fusion.1
  25.7 0.1 select_add_fusion
  25.9 6.8 %collective-permute-done.2 = f32[16,2,2,1024]{3,0,2,1:T(8,128)} collective-permute-done((f32[16,2,2,1024]{3,0,2,1:T(8,128)}, f32[16,2,2,1024]{3,0,2,1:T(8,128)}, u32[]{:S(2)}, u32[]{:S(2)}) %collective-permute-start.2) | collective-permute-done | bytes 262176 | tf_op jit(solution)/shard_map/ppermute | solution.py:25
  32.6 1.0 constant_dynamic-update-slice_fusion.2
  33.6 0.0 copy-done
  33.6 2.1 %subtract_multiply_fusion.3 = (f32[16,2,16,1024]{3,0,2,1:T(8,128)S(1)}, f32[16,2,20,1024]{3,0,2,1:T(8,128)S(1)}, f32[16,2,16,1024]{3,0,2,1:T(8,128)S(1)}) fusion(f32[16,2,16,1023]{3,0,2,1:T(8,128)S(1)} %slice.322, f32[16,1024]{1,0:T(8,128)S(1)} %get-tuple-element.47, f32[16,2,16,1024]{3,2,1,0:T(8,128)S(1)} %copy-done, ...), kind=kLoop, calls=%fused_computation.30 | loop fusion | flops 2097152 | bytes 12713984 | tf_op jit(solution)/shard_map/mul | solution.py:76
  35.7 0.2 collective-permute-done.3
  35.9 0.3 slice_subtract_fusion.1
  36.3 4.4 %fusion.8 = f32[16,2,16,1024]{3,0,2,1:T(8,128)S(1)} fusion(f32[16,2,19,1024]{3,0,2,1:T(8,128)S(1)} %slice_subtract_fusion.1, f32[16,2,16,992]{3,0,2,1:T(8,128)S(1)} %bitcast.347, f32[16,2,16,1024]{3,0,2,1:T(8,128)S(1)} %get-tuple-element.29, f32[16,2,16,1024]{3,0,2,1:T(8,128)S(1)} %get-tuple-element.27, f32[16,2,16,1023]{3,0,2,1:T(8,128)S(1)} %bitcast.346, ...), kind=kLoop, calls=%fused_computation.20 | loop fusion | flops 6291456 | bytes 21166080 | tf_op jit(solution)/shard_map/add | solution.py:137
  40.7 0.0 copy-start.1
  40.7 1.3 %copy-done.1 = f32[16,2,16,1024]{3,0,2,1:T(8,128)} copy-done((f32[16,2,16,1024]{3,0,2,1:T(8,128)}, f32[16,2,16,1024]{3,0,2,1:T(8,128)S(1)}, u32[]{:S(2)}) %copy-start.1) | copy-done | bytes 2097176
  42.0 0.6 slice.357
  42.6 0.0 copy-start.2
  42.6 28.3 %all-gather.2.cloned.1.call-done = f32[16,2,16,1024]{3,2,1,0:T(8,128)} async-done(((f32[1,2,16,1024]{3,2,1,0:T(8,128)}), f32[16,2,16,1024]{3,2,1,0:T(8,128)}) %all-gather.2.cloned.1.call-update) | async-done | bytes 2097168 | tf_op jit(solution)/shard_map/all_gather | solution.py:36
  70.9 1.7 %reduce_sum.9 = f32[2,16,1024]{2,1,0:T(8,128)S(1)} reduce(f32[16,2,16,1024]{3,2,1,0:T(8,128)} %all-gather.2.cloned.1.call-done, f32[]{:T(128)} %constant.118.clone.1), dimensions={0}, to_apply=%region_0.1 | reduce | flops 491520 | bytes 2228228 | tf_op jit(solution)/shard_map/reduce_sum | solution.py:36
  72.7 0.1 slice.346
  72.8 0.1 slice.344
  72.9 0.5 collective-permute-start.4
  73.4 3.3 %collective-permute-start.5 = (f32[2,2,1024]{2,1,0:T(2,128)S(1)}, f32[2,2,1024]{2,1,0:T(2,128)S(1)}, u32[]{:S(2)}, u32[]{:S(2)}) collective-permute-start(f32[2,2,1024]{2,1,0:T(2,128)S(1)} %get-tuple-element.46), channel_id=1, source_target_pairs={{16,0},{32,16},{48,32},{64,48},{80,64},{96,80},{112,96},{128,112},... | collective-permute-start | bytes 49160 | tf_op jit(solution)/shard_map/ppermute | solution.py:27
  76.7 0.0 copy-done.2
  76.8 0.1 add_bitcast_fusion.1
  76.9 0.9 collective-permute-done.4
  77.8 0.0 collective-permute-done.5
  77.8 0.1 fusion.14
  77.9 0.1 fusion.20
  78.1 0.1 slice_bitcast_fusion.6
  78.2 0.1 add_bitcast_fusion
  78.2 0.1 maximum_bitcast_fusion
  78.3 0.1 add_bitcast_fusion.3
  78.5 1.0 slice_add_fusion.1
  79.5 0.2 fusion.11
  79.7 0.7 fusion
  80.4 1.3 %collective-permute-start.6 = (f32[16,2,2,1024]{3,0,2,1:T(8,128)S(1)}, f32[16,2,2,1024]{3,0,2,1:T(8,128)S(1)}, u32[]{:S(2)}, u32[]{:S(2)}) collective-permute-start(f32[16,2,2,1024]{3,0,2,1:T(8,128)S(1)} %get-tuple-element.25), channel_id=1, source_target_pairs={{0,16},{16,32},{32,48},{48,64},{64,80},{80,96},{96,112},{112,128},... | collective-permute-start | bytes 786440 | tf_op jit(solution)/shard_map/ppermute | solution.py:25
  81.7 2.4 %collective-permute-start.7 = (f32[16,2,2,1024]{3,0,2,1:T(8,128)S(1)}, f32[16,2,2,1024]{3,0,2,1:T(8,128)S(1)}, u32[]{:S(2)}, u32[]{:S(2)}) collective-permute-start(f32[16,2,2,1024]{3,0,2,1:T(8,128)S(1)} %get-tuple-element.26), channel_id=1, source_target_pairs={{16,0},{32,16},{48,32},{64,48},{80,64},{96,80},{112,96},{128,112},... | collective-permute-start | bytes 786440 | tf_op jit(solution)/shard_map/ppermute | solution.py:27
  84.1 0.9 subtract_multiply_fusion.1
  85.0 0.1 select_add_fusion.1
  85.1 7.2 %collective-permute-done.6 = f32[16,2,2,1024]{3,0,2,1:T(8,128)S(1)} collective-permute-done((f32[16,2,2,1024]{3,0,2,1:T(8,128)S(1)}, f32[16,2,2,1024]{3,0,2,1:T(8,128)S(1)}, u32[]{:S(2)}, u32[]{:S(2)}) %collective-permute-start.6) | collective-permute-done | bytes 262176 | tf_op jit(solution)/shard_map/ppermute | solution.py:25
  92.3 2.4 %collective-permute-done.7 = f32[16,2,2,1024]{3,0,2,1:T(8,128)S(1)} collective-permute-done((f32[16,2,2,1024]{3,0,2,1:T(8,128)S(1)}, f32[16,2,2,1024]{3,0,2,1:T(8,128)S(1)}, u32[]{:S(2)}, u32[]{:S(2)}) %collective-permute-start.7) | collective-permute-done | bytes 262176 | tf_op jit(solution)/shard_map/ppermute | solution.py:27
  94.7 0.6 pad_maximum_fusion.1
  95.3 0.2 slice_subtract_fusion
  95.5 2.7 %fusion.3 = f32[16,2,16,1024]{3,0,2,1:T(8,128)S(1)} fusion(f32[16,2,19,1024]{3,0,2,1:T(8,128)S(1)} %slice_subtract_fusion, f32[16,2,16,992]{3,0,2,1:T(8,128)S(1)} %bitcast.348, f32[16,2,16,1024]{3,0,2,1:T(8,128)S(1)} %get-tuple-element.23, f32[16,2,16,1023]{3,0,2,1:T(8,128)S(1)} %bitcast.345, f32[16,2,16,992]{3,0,2,1:T(8,128)S(1)} %slice.357, ...), kind=kLoop, calls=%fused_computation.11 | loop fusion | flops 7864320 | bytes 19134464 | tf_op jit(solution)/shard_map/add | solution.py:137
  98.3 0.6 slice.374
  98.9 0.6 pad_maximum_fusion.2
  99.6 2.5 %copy.20 = f32[16,2,16,1024]{3,2,1,0:T(8,128)} copy(f32[16,2,16,1024]{3,0,2,1:T(8,128)S(1)} %pad_maximum_fusion.2) | data formatting | bytes 4194304 | tf_op jit(solution)/shard_map/concatenate | solution.py:140
  (21 shorter events, 0.4 us)
Async XLA Ops:
  6.5 64.4 %all-gather.2.cloned.1.call-start = ((), (), s32[]{:S(2)}) async-start(), calls=%async_computation | async-start | bytes 2228224 | tf_op jit(solution)/shard_map/all_gather | solution.py:36
  11.3 13.8 %collective-permute-start = (f32[2,3168]{1,0:T(2,128)S(1)}, f32[2,3168]{1,0:T(2,128)S(1)}, u32[]{:S(2)}, u32[]{:S(2)}) collective-permute-start(f32[2,3168]{1,0:T(2,128)S(1)} %get-tuple-element.39), channel_id=1, source_target_pairs={{0,16},{16,32},{32,48},{48,64},{64,80},{80,96},{96,112},{112,128},... | collective-permute-start | bytes 76040 | tf_op jit(solution)/shard_map/ppermute | solution.py:25
  13.4 11.7 %collective-permute-start.1 = (f32[2,3168]{1,0:T(2,128)S(1)}, f32[2,3168]{1,0:T(2,128)S(1)}, u32[]{:S(2)}, u32[]{:S(2)}) collective-permute-start(f32[2,3168]{1,0:T(2,128)S(1)} %get-tuple-element.40), channel_id=1, source_target_pairs={{16,0},{32,16},{48,32},{64,48},{80,64},{96,80},{112,96},{128,112},... | collective-permute-start | bytes 76040 | tf_op jit(solution)/shard_map/ppermute | solution.py:27
  22.5 13.5 %collective-permute-start.3 = (f32[16,2,2,1024]{3,0,2,1:T(8,128)}, f32[16,2,2,1024]{3,0,2,1:T(8,128)S(1)}, u32[]{:S(2)}, u32[]{:S(2)}) collective-permute-start(f32[16,2,2,1024]{3,0,2,1:T(8,128)} %get-tuple-element.30), channel_id=1, source_target_pairs={{16,0},{32,16},{48,32},{64,48},{80,64},{96,80},{112,96},{128,112},... | collective-permute-start | bytes 786440 | tf_op jit(solution)/shard_map/ppermute | solution.py:27
  23.8 8.8 %collective-permute-start.2 = (f32[16,2,2,1024]{3,0,2,1:T(8,128)}, f32[16,2,2,1024]{3,0,2,1:T(8,128)}, u32[]{:S(2)}, u32[]{:S(2)}) collective-permute-start(f32[16,2,2,1024]{3,0,2,1:T(8,128)} %get-tuple-element.31), channel_id=1, source_target_pairs={{0,16},{16,32},{32,48},{48,64},{64,80},{80,96},{96,112},{112,128},... | collective-permute-start | bytes 786440 | tf_op jit(solution)/shard_map/ppermute | solution.py:25
  25.4 8.2 %copy-start = (f32[16,2,16,1024]{3,2,1,0:T(8,128)S(1)}, f32[16,2,16,1024]{3,2,1,0:T(8,128)}, u32[]{:S(2)}) copy-start(f32[16,2,16,1024]{3,2,1,0:T(8,128)} %param.9) | copy-start | bytes 6291460
  40.7 1.3 %copy-start.1 = (f32[16,2,16,1024]{3,0,2,1:T(8,128)}, f32[16,2,16,1024]{3,0,2,1:T(8,128)S(1)}, u32[]{:S(2)}) copy-start(f32[16,2,16,1024]{3,0,2,1:T(8,128)S(1)} %fusion.8) | copy-start | bytes 6291460
  42.6 34.1 %copy-start.2 = (f32[16,32]{1,0:T(8,128)S(1)}, f32[16,32]{1,0:T(8,128)}, u32[]{:S(2)}) copy-start(f32[16,32]{1,0:T(8,128)} %param.15) | copy-start | bytes 6148
  72.9 5.0 %collective-permute-start.4 = (f32[2,2,1024]{2,1,0:T(2,128)S(1)}, f32[2,2,1024]{2,1,0:T(2,128)S(1)}, u32[]{:S(2)}, u32[]{:S(2)}) collective-permute-start(f32[2,2,1024]{2,1,0:T(2,128)S(1)} %get-tuple-element.45), channel_id=1, source_target_pairs={{0,16},{16,32},{32,48},{48,64},{64,80},{80,96},{96,112},{112,128},... | collective-permute-start | bytes 49160 | tf_op jit(solution)/shard_map/ppermute | solution.py:25
  73.4 4.4 %collective-permute-start.5 = (f32[2,2,1024]{2,1,0:T(2,128)S(1)}, f32[2,2,1024]{2,1,0:T(2,128)S(1)}, u32[]{:S(2)}, u32[]{:S(2)}) collective-permute-start(f32[2,2,1024]{2,1,0:T(2,128)S(1)} %get-tuple-element.46), channel_id=1, source_target_pairs={{16,0},{32,16},{48,32},{64,48},{80,64},{96,80},{112,96},{128,112},... | collective-permute-start | bytes 49160 | tf_op jit(solution)/shard_map/ppermute | solution.py:27
  80.4 11.9 %collective-permute-start.6 = (f32[16,2,2,1024]{3,0,2,1:T(8,128)S(1)}, f32[16,2,2,1024]{3,0,2,1:T(8,128)S(1)}, u32[]{:S(2)}, u32[]{:S(2)}) collective-permute-start(f32[16,2,2,1024]{3,0,2,1:T(8,128)S(1)} %get-tuple-element.25), channel_id=1, source_target_pairs={{0,16},{16,32},{32,48},{48,64},{64,80},{80,96},{96,112},{112,128},... | collective-permute-start | bytes 786440 | tf_op jit(solution)/shard_map/ppermute | solution.py:25
  81.7 13.0 %collective-permute-start.7 = (f32[16,2,2,1024]{3,0,2,1:T(8,128)S(1)}, f32[16,2,2,1024]{3,0,2,1:T(8,128)S(1)}, u32[]{:S(2)}, u32[]{:S(2)}) collective-permute-start(f32[16,2,2,1024]{3,0,2,1:T(8,128)S(1)} %get-tuple-element.26), channel_id=1, source_target_pairs={{16,0},{32,16},{48,32},{64,48},{80,64},{96,80},{112,96},{128,112},... | collective-permute-start | bytes 786440 | tf_op jit(solution)/shard_map/ppermute | solution.py:27
Sparse Core Ops, SparseCore 0:
  10.1 60.7 all-gather.1
